TPU v7x, 32 devices: a whole 2x2x4 slice. The times are simulated.
32 devices in a mesh: row: 4 (over y, x), col: 4 (over z), pts: 2 (over core).
Axes of the slice: x: 2, y: 2, z: 4, core: 2. Of those that a mesh axis runs over, the one named last changes fastest.
Arguments:
- green_panel: bfloat16 [4, 2, 512, 6144], P(None, None, 'col', 'pts'), may hold values from -6 to 6
- log_psd: float32 [2, 4, 3072], P('pts', None, ('row', 'col')), may hold values from -1.1 to 1.1
- observed: float32 [4, 2, 512, 512], P(None, None, 'row', 'col'), may hold values from -1 to 1
- pair_weights: int32 [512, 512], P('row', 'col'), may hold values from 0 to 4, as said below
Outputs:
- updated_log_psd: float32 [2, 4, 3072], P('pts', None, ('row', 'col'))
Inputs may be any that keep to these rules, and one draw needn't show every extreme that they name: pair_weights is 0 for pairs that are not listed and for every station paired with itself; the share of listed pairs differs from one block of 128 x 128 pairs (one index of row by one of col) to another, and some such blocks list no pair.
All inputs are finite; a program needn't handle non-finite values.
Results may differ from a plain program's by a relative error of at most 0.0014.
Values may be sent and summed in bfloat16 or wider, within the bound.
No kernel may reach another device: no remote copies, remote signals or barrier semaphores. Data moves between devices by JAX's collectives and lax.ppermute only.
A program may use at most 64 MiB of HBM per device.

v0:
```python
import jax
import jax.numpy as jnp
from jax import lax
from jax.sharding import PartitionSpec as P

ITERS = 2
epsilon = 1e-06
descent = 0.1


def from_root(block, axis, source):
    block = jnp.where(lax.axis_index(axis) == source, block, jnp.zeros_like(block))
    return lax.psum(block, axis)


def pair_total(partial_value):
    return lax.psum(partial_value.astype(jnp.bfloat16), "pts").astype(jnp.float32)


def descend(log_field, gradient, entry_count):
    squares = lax.psum(jnp.sum(gradient * gradient), ("row", "col", "pts"))
    return log_field - descent * gradient / jnp.sqrt(squares / entry_count + epsilon)


def correlate(left_rows, weighted):
    half_a = left_rows.shape[1] // 2
    half_b = weighted.shape[1] // 2
    products = jnp.einsum("fan,fbn->fab", left_rows, weighted, preferred_element_type=jnp.float32)
    corr_real = products[:, :half_a, :half_b] + products[:, half_a:, half_b:]
    corr_imag = products[:, half_a:, :half_b] - products[:, :half_a, half_b:]
    return jnp.stack([corr_real, corr_imag], axis=1)


def adjoint_block(adjoint):
    adj_real = adjoint[:, 0]
    adj_imag = adjoint[:, 1]
    top_half = jnp.concatenate([adj_real, -adj_imag], axis=2)
    low_half = jnp.concatenate([adj_imag, adj_real], axis=2)
    return jnp.concatenate([top_half, low_half], axis=1)


def point_terms(adjoint, right_rows, left_rows, psd_field, quad_weight):
    accumulated = jnp.einsum(
        "fab,fbn->fan", adjoint_block(adjoint), right_rows, preferred_element_type=jnp.float32
    )
    return quad_weight * psd_field * jnp.sum(left_rows * accumulated, axis=1)


def body(green_panel, log_psd, observed, pair_weights):
    freq_count, comp_count, span_j, local_pts = green_panel.shape
    span_i = observed.shape[2]
    row_count = lax.axis_size("row")
    col_count = lax.axis_size("col")
    pts_count = lax.axis_size("pts")
    quad_weight = 1.0 / (pts_count * local_pts)
    entry_count = freq_count * pts_count * local_pts
    pair_scale = pair_weights.astype(jnp.float32)
    log_start = log_psd[0]
    group_ratio = col_count // row_count
    pieces = []
    for member in range(group_ratio):
        pieces.append(from_root(green_panel, "col", lax.axis_index("row") * group_ratio + member))
    rows_block = jnp.concatenate(pieces, axis=2).reshape(freq_count, 2 * span_i, local_pts)
    cols_block = green_panel.reshape(freq_count, 2 * span_j, local_pts)

    def run_sweep(sweep_idx, log_field):
        whole_log = lax.all_gather(log_field, ("row", "col"), axis=1, tiled=True)
        psd_field = jnp.exp(whole_log)
        weighted = (green_panel * psd_field[:, None, None, :]).astype(jnp.bfloat16)
        weighted = weighted.reshape(freq_count, 2 * span_j, local_pts)
        partial_value = correlate(rows_block, weighted)
        pair_sum = pair_total(partial_value)
        adjoint = (pair_scale * (quad_weight * pair_sum - observed)).astype(jnp.bfloat16)
        point_part = point_terms(adjoint, cols_block, rows_block, psd_field, quad_weight)
        gradient = lax.psum_scatter(point_part, ("row", "col"), scatter_dimension=1, tiled=True)
        return descend(log_field, gradient, entry_count)

    log_final = lax.fori_loop(0, ITERS, run_sweep, log_start)
    return log_final[None]


def solution(mesh):
    return jax.shard_map(
        body,
        mesh=mesh,
        in_specs=(
            P(None, None, "col", "pts"),
            P("pts", None, ("row", "col")),
            P(None, None, "row", "col"),
            P("row", "col"),
        ),
        out_specs=P("pts", None, ("row", "col")),
        check_vma=False,
    )
```

profile of v0, /device:TPU:0, one launch (start us, length us, event | category | flops | bytes accessed | tf_op | source)
XLA Modules:
  0.0 727.3 jit_solution(13803645193533125202)
XLA Ops:
  6.5 5.8 broadcast_select_fusion
  12.4 1.0 copy-done
  13.8 224.4 %all-reduce.3.cloned.1.call-done = bf16[4,256,3072]{2,1,0:T(8,128)(2,1)} async-done(((bf16[4,256,3072]{2,1,0:T(8,128)(2,1)}), bf16[4,256,3072]{2,1,0:T(8,128)(2,1)}) %all-reduce.3.cloned.1.call-update) | async-done | bytes 6291472 | tf_op jit(solution)/shard_map/psum | solution.py:13
  238.1 482.1 %while.10 = (s32[]{:T(128)}, f32[4,192]{1,0:T(4,128)S(1)}, bf16[4,256,3072]{2,1,0:T(8,128)(2,1)}, f32[128,128]{0,1:T(8,128)S(1)}, bf16[4,2,128,3072]{3,2,1,0:T(8...) while((s32[]{:T(128)}, f32[4,192]{1,0:T(4,128)S(1)}, ...), condition=%wide.region_7.8_spmd, body=%wide.region_1.7_spmd.sunk | while | flops 3243458304 | bytes 34303204 | solution.py:78
  238.2 39.0 %all-gather.2 = f32[16,192,4]{1,2,0:T(4,128)S(1)} all-gather(f32[1,192,4]{1,2,0:T(4,128)S(1)} %bitcast.59), channel_id=1, replica_groups=mesh['row'=4,'col'=4,'pts'=2] {'row','col'}, dimensions={0}, use_global_device_ids=true | all-gather | bytes 52224 | tf_op jit(solution)/shard_map/while/body/eval_jaxpr/all_gather | solution.py:67
  277.2 6.4 fusion.33
  283.7 0.7 pad_maximum_fusion.2
  284.6 14.6 %all-reduce.5.cloned.1.call-done = bf16[4,2,128,128]{2,3,0,1:T(8,128)(2,1)} async-done(((bf16[4,2,128,128]{2,3,0,1:T(8,128)(2,1)}), bf16[4,2,128,128]{2,3,0,1:T(8,128)(2,1)}) %all-reduce.5.cloned.1.call-update) | async-done | bytes 262160 | tf_op jit(solution)/shard_map/while/body/eval_jaxpr/psum | solution.py:17
  299.2 1.0 multiply_convert_fusion.2
  300.3 6.8 multiply_reduce_fusion.4
  307.1 1.7 copy.28
  308.8 127.5 %reduce-scatter.6.cloned.1.call-done = f32[192,4]{1,0:T(8,128)} async-done(((f32[3072,4]{1,0:T(8,128)}), f32[192,4]{1,0:T(8,128)}) %reduce-scatter.6.cloned.1.call-update) | async-done | bytes 3088 | tf_op jit(solution)/shard_map/while
  436.3 1.0 copy.29
  437.9 40.0 %psum.25 = f32[]{:T(128)} all-reduce(f32[]{:T(128)} %multiply_reduce_fusion.5), channel_id=1, replica_groups=mesh['row'=4,'col'=4,'pts'=2] {'row','col','pts'}, use_global_device_ids=true, to_apply=%region_6.6 | all-reduce | flops 1 | bytes 8 | tf_op jit(solution)/shard_map/while/body/eval_jaxpr/psum | solution.py:21
  478.6 39.4 %all-gather.2 = f32[16,192,4]{1,2,0:T(4,128)S(1)} all-gather(f32[1,192,4]{1,2,0:T(4,128)S(1)} %bitcast.59), channel_id=1, replica_groups=mesh['row'=4,'col'=4,'pts'=2] {'row','col'}, dimensions={0}, use_global_device_ids=true | all-gather | bytes 52224 | tf_op jit(solution)/shard_map/while/body/eval_jaxpr/all_gather | solution.py:67
  518.2 6.4 fusion.33
  524.7 0.7 pad_maximum_fusion.2
  525.5 15.4 %all-reduce.5.cloned.1.call-done = bf16[4,2,128,128]{2,3,0,1:T(8,128)(2,1)} async-done(((bf16[4,2,128,128]{2,3,0,1:T(8,128)(2,1)}), bf16[4,2,128,128]{2,3,0,1:T(8,128)(2,1)}) %all-reduce.5.cloned.1.call-update) | async-done | bytes 262160 | tf_op jit(solution)/shard_map/while/body/eval_jaxpr/psum | solution.py:17
  540.9 1.0 multiply_convert_fusion.2
  542.0 6.8 multiply_reduce_fusion.4
  548.8 1.7 copy.28
  550.4 127.5 %reduce-scatter.6.cloned.1.call-done = f32[192,4]{1,0:T(8,128)} async-done(((f32[3072,4]{1,0:T(8,128)}), f32[192,4]{1,0:T(8,128)}) %reduce-scatter.6.cloned.1.call-update) | async-done | bytes 3088 | tf_op jit(solution)/shard_map/while
  677.9 1.0 copy.29
  679.5 40.0 %psum.25 = f32[]{:T(128)} all-reduce(f32[]{:T(128)} %multiply_reduce_fusion.5), channel_id=1, replica_groups=mesh['row'=4,'col'=4,'pts'=2] {'row','col','pts'}, use_global_device_ids=true, to_apply=%region_6.6 | all-reduce | flops 1 | bytes 8 | tf_op jit(solution)/shard_map/while/body/eval_jaxpr/psum | solution.py:21
  (36 shorter events, 2.8 us)
Async XLA Ops:
  6.5 231.6 %all-reduce.3.cloned.1.call-start = ((), (), s32[]{:S(2)}) async-start(), calls=%async_computation.1 | async-start | bytes 12582912 | tf_op jit(solution)/shard_map/psum | solution.py:13
  12.4 1.0 copy-start
  12.4 1.2 copy-start.3
  12.4 225.8 %copy-start.2 = (f32[1,4,192]{2,1,0:T(4,128)S(1)}, f32[1,4,192]{2,1,0:T(4,128)}, u32[]{:S(2)}) copy-start(f32[1,4,192]{2,1,0:T(4,128)} %param.7) | copy-start | bytes 9220
  238.1 61.0 %all-reduce.5.cloned.1.call-start = ((), (), s32[]{:S(2)}) async-start(), calls=%async_computation.2 | async-start | bytes 524288 | tf_op jit(solution)/shard_map/while/body/eval_jaxpr/psum | solution.py:17
  284.5 151.8 %reduce-scatter.6.cloned.1.call-start = ((), (), s32[]{:S(2)}) async-start(), calls=%async_computation.3 | async-start | bytes 1671168 | tf_op jit(solution)/shard_map/while
  478.6 62.3 %all-reduce.5.cloned.1.call-start = ((), (), s32[]{:S(2)}) async-start(), calls=%async_computation.2 | async-start | bytes 524288 | tf_op jit(solution)/shard_map/while/body/eval_jaxpr/psum | solution.py:17
  525.4 152.5 %reduce-scatter.6.cloned.1.call-start = ((), (), s32[]{:S(2)}) async-start(), calls=%async_computation.3 | async-start | bytes 1671168 | tf_op jit(solution)/shard_map/while
  720.2 0.6 copy-start.1
Sparse Core Ops, SparseCore 0:
  12.5 225.5 all-reduce.2
  284.6 14.5 all-reduce.4
  308.9 127.3 reduce-scatter.5
  525.5 15.2 all-reduce.4
  550.6 127.3 reduce-scatter.5
where the time goes:
time: 728 us; the launch traced here: 727 us
  waiting for transfers between devices  510 us (70%)
  blocking collectives  158 us (22%)
  matrix products  26.4 us (4%)
  between operations  13.1 us (2%)
  other arithmetic  10.9 us (1%)
  local copies, waits for them, and re-layouts  7.41 us (1%)
    while x6, waiting for transfers between devices  255 us
    psum x1, waiting for transfers between devices, from_root(): return lax.psum(block, axis)  224 us
    psum x2, blocking collectives, descend(): squares = lax.psum(jnp.sum(gradient * gradient), ('row', 'col', 'pts'))  80.1 us
    all_gather x2, blocking collectives, run_sweep(): whole_log = lax.all_gather(log_field, ('row', 'col'), axis=1, tiled=True)  78.4 us
    psum x2, waiting for transfers between devices, pair_total(): lax.psum(partial_value.astype(jnp.bfloat16), 'pts').astype(jnp.float32)  30 us
  transfers between devices with their start and end apart: 5, of which 5 were waited for; matrix products, arithmetic and copies ran while one was open for 0% of the time, Pallas kernels for 0%

commit v1 on v0

--- a/solution.py
+++ b/solution.py
@@ -14,7 +14,9 @@
 
 
 def pair_total(partial_value):
-    return lax.psum(partial_value.astype(jnp.bfloat16), "pts").astype(jnp.float32)
+    return jnp.sum(lax.all_gather(partial_value.astype(jnp.bfloat16), "pts"), axis=0).astype(
+        jnp.float32
+    )
 
 
 def descend(log_field, gradient, entry_count):

time: 728 us -> 690 us (0.948)
  waiting for transfers between devices: 510 us -> 470 us
    psum x2 -> x0, waiting for transfers between devices: 30 us -> none  [pair_total(): lax.psum(partial_value.astype(jnp.bfloat16), 'pts').astype(jnp.float32)]
    while x6 -> x4, waiting for transfers between devices: 255 us -> 246 us
  transfers between devices with their start and end apart: 5 -> 3, of which waited for: 5 -> 3; matrix products, arithmetic and copies ran while one was open for 0% -> 0% of each run, Pallas kernels for 0% -> 0%
where the time goes in v1:
time: 690 us; the launch traced here: 689 us
  waiting for transfers between devices  470 us (68%)
  blocking collectives  163 us (24%)
  matrix products  25.8 us (4%)
  between operations  13.1 us (2%)
  other arithmetic  7.81 us (1%)
  local copies, waits for them, and re-layouts  7.51 us (1%)
    while x4, waiting for transfers between devices  246 us
    psum x1, waiting for transfers between devices, from_root(): return lax.psum(block, axis)  225 us
    psum x2, blocking collectives, descend(): squares = lax.psum(jnp.sum(gradient * gradient), ('row', 'col', 'pts'))  80.1 us
    all_gather x2, blocking collectives, run_sweep(): whole_log = lax.all_gather(log_field, ('row', 'col'), axis=1, tiled=True)  78.4 us
  transfers between devices with their start and end apart: 3, of which 3 were waited for; matrix products, arithmetic and copies ran while one was open for 0% of the time, Pallas kernels for 0%

profile of v1, /device:TPU:0, one launch (start us, length us, event | category | flops | bytes accessed | tf_op | source)
XLA Modules:
  0.0 689.1 jit_solution(1262105276398051565)
XLA Ops:
  6.5 5.8 broadcast_select_fusion
  12.4 1.0 copy-done
  13.5 224.7 %all-reduce.2.cloned.1.call-done = bf16[4,256,3072]{2,1,0:T(8,128)(2,1)} async-done(((bf16[4,256,3072]{2,1,0:T(8,128)(2,1)}), bf16[4,256,3072]{2,1,0:T(8,128)(2,1)}) %all-reduce.2.cloned.1.call-update) | async-done | bytes 6291472 | tf_op jit(solution)/shard_map/psum | solution.py:13
  238.1 443.8 %while.12 = (s32[]{:T(128)}, f32[4,192]{1,0:T(4,128)S(1)}, bf16[4,256,3072]{2,1,0:T(8,128)(2,1)}, f32[128,128]{1,0:T(8,128)S(1)}, bf16[4,2,128,3072]{3,2,1,0:T(8...) while((s32[]{:T(128)}, f32[4,192]{1,0:T(4,128)S(1)}, ...), condition=%wide.region_7.8_spmd, body=%wide.region_1.7_spmd.sunk | while | flops 3243458304 | bytes 34827464 | solution.py:80
  238.2 39.0 %all-gather.2 = f32[16,192,4]{1,2,0:T(4,128)S(1)} all-gather(f32[1,192,4]{1,2,0:T(4,128)S(1)} %bitcast.59), channel_id=1, replica_groups=mesh['row'=4,'col'=4,'pts'=2] {'row','col'}, dimensions={0}, use_global_device_ids=true | all-gather | bytes 52224 | tf_op jit(solution)/shard_map/while/body/eval_jaxpr/all_gather | solution.py:69
  277.2 6.4 fusion.33
  283.8 0.2 copy.34
  284.0 2.2 all_gather.14
  286.4 6.4 multiply_reduce_fusion.4
  292.9 1.7 copy.35
  294.6 122.6 %reduce-scatter.6.cloned.1.call-done = f32[192,4]{1,0:T(8,128)} async-done(((f32[3072,4]{1,0:T(8,128)}), f32[192,4]{1,0:T(8,128)}) %reduce-scatter.6.cloned.1.call-update) | async-done | bytes 3088 | tf_op jit(solution)/shard_map/while
  417.2 1.0 copy.36
  418.1 0.6 multiply_reduce_fusion.5
  418.7 40.1 %psum.19 = f32[]{:T(128)} all-reduce(f32[]{:T(128)} %multiply_reduce_fusion.5), channel_id=1, replica_groups=mesh['row'=4,'col'=4,'pts'=2] {'row','col','pts'}, use_global_device_ids=true, to_apply=%region_6.6 | all-reduce | flops 1 | bytes 8 | tf_op jit(solution)/shard_map/while/body/eval_jaxpr/psum | solution.py:23
  459.6 39.5 %all-gather.2 = f32[16,192,4]{1,2,0:T(4,128)S(1)} all-gather(f32[1,192,4]{1,2,0:T(4,128)S(1)} %bitcast.59), channel_id=1, replica_groups=mesh['row'=4,'col'=4,'pts'=2] {'row','col'}, dimensions={0}, use_global_device_ids=true | all-gather | bytes 52224 | tf_op jit(solution)/shard_map/while/body/eval_jaxpr/all_gather | solution.py:69
  499.1 6.4 fusion.33
  505.9 2.2 all_gather.14
  508.3 6.4 multiply_reduce_fusion.4
  514.8 1.7 copy.35
  516.5 123.2 %reduce-scatter.6.cloned.1.call-done = f32[192,4]{1,0:T(8,128)} async-done(((f32[3072,4]{1,0:T(8,128)}), f32[192,4]{1,0:T(8,128)}) %reduce-scatter.6.cloned.1.call-update) | async-done | bytes 3088 | tf_op jit(solution)/shard_map/while
  639.7 1.0 copy.36
  640.6 0.6 multiply_reduce_fusion.5
  641.3 40.0 %psum.19 = f32[]{:T(128)} all-reduce(f32[]{:T(128)} %multiply_reduce_fusion.5), channel_id=1, replica_groups=mesh['row'=4,'col'=4,'pts'=2] {'row','col','pts'}, use_global_device_ids=true, to_apply=%region_6.6 | all-reduce | flops 1 | bytes 8 | tf_op jit(solution)/shard_map/while/body/eval_jaxpr/psum | solution.py:23
  681.9 0.6 copy-done.1
  (35 shorter events, 1.3 us)
Async XLA Ops:
  6.5 231.6 %all-reduce.2.cloned.1.call-start = ((), (), s32[]{:S(2)}) async-start(), calls=%async_computation.1 | async-start | bytes 12582912 | tf_op jit(solution)/shard_map/psum | solution.py:13
  12.4 1.0 copy-start
  12.4 1.1 copy-start.3
  12.4 225.8 %copy-start.2 = (f32[1,4,192]{2,1,0:T(4,128)S(1)}, f32[1,4,192]{2,1,0:T(4,128)}, u32[]{:S(2)}) copy-start(f32[1,4,192]{2,1,0:T(4,128)} %param.7) | copy-start | bytes 9220
  238.1 179.0 %reduce-scatter.6.cloned.1.call-start = ((), (), s32[]{:S(2)}) async-start(), calls=%async_computation.2 | async-start | bytes 1671168 | tf_op jit(solution)/shard_map/while
  459.5 180.2 %reduce-scatter.6.cloned.1.call-start = ((), (), s32[]{:S(2)}) async-start(), calls=%async_computation.2 | async-start | bytes 1671168 | tf_op jit(solution)/shard_map/while
  681.9 0.6 copy-start.1
Sparse Core Ops, SparseCore 0:
  12.5 225.5 all-reduce.1
  294.7 122.4 reduce-scatter.5
  516.6 123.0 reduce-scatter.5
